TPU v7x, 256 devices: a whole 4x4x8 slice. The times are simulated.
256 devices in a mesh: row: 8 (over z), col: 32 (over y, x, core).
Axes of the slice: x: 4, y: 4, z: 8, core: 2. Of those that a mesh axis runs over, the one named last changes fastest.
Arguments:
- tokens: bfloat16 [512, 8192], P('col', 'row'), may hold values from -6 to 6
- cotangent: bfloat16 [512, 8192], P('col', 'row'), may hold values from -6 to 6
- w_gate: bfloat16 [8192, 16384], P('row', 'col'), may hold values from -0.09375 to 0.09375
- w_up: bfloat16 [8192, 16384], P('row', 'col'), may hold values from -0.09375 to 0.09375
- w_down: bfloat16 [16384, 8192], P('col', 'row'), may hold values from -0.0625 to 0.0625
- order_gate: int32 [2048], replicated, may hold values from 0 to 2047, each once
- order_up: int32 [2048], replicated, may hold values from 0 to 2047, each once
- order_down: int32 [2048], replicated, may hold values from 0 to 2047, each once
Outputs:
- output: bfloat16 [512, 8192], P('col', 'row')
- input_grad: bfloat16 [512, 8192], P('col', 'row')
- gate_weight_grad: float32 [8192, 16384], P('row', 'col')
- up_weight_grad: float32 [8192, 16384], P('row', 'col')
- down_weight_grad: float32 [16384, 8192], P('col', 'row')
Inputs may be any that keep to these rules, and one draw needn't show every extreme that they name: `order_gate`: each of the 2048 block numbers appears exactly once. `order_up`: each of the 2048 block numbers appears exactly once. `order_down`: each of the 2048 block numbers appears exactly once.
All inputs are finite; a program needn't handle non-finite values.
Results may differ from a plain program's by a relative error of at most 0.0049.
Values may be sent and summed in bfloat16 or wider, within the bound.
No kernel may reach another device: no remote copies, remote signals or barrier semaphores. Data moves between devices by JAX's collectives and lax.ppermute only.
A program may use at most 64 MiB of HBM per device.

v0:
```python
import jax
import jax.numpy as jnp
from jax import lax
from jax.sharding import PartitionSpec as P

BLOCK = 256


def kept_table(order, row_first, col_first, row_count, col_count, stride):
    kept_count = order.shape[0] // 2
    row_ids = row_first + jnp.arange(row_count, dtype=jnp.int32)
    col_ids = col_first + jnp.arange(col_count, dtype=jnp.int32)
    block_ids = row_ids[:, None] * stride + col_ids[None, :]
    return jnp.any(block_ids[:, :, None] == order[:kept_count][None, None, :], axis=2)


def expand_mask(kept_mask):
    row_count, col_count = kept_mask.shape
    spread = jnp.broadcast_to(kept_mask[:, None, :, None], (row_count, BLOCK, col_count, BLOCK))
    return spread.reshape(row_count * BLOCK, col_count * BLOCK)


def dense_apply(left_operand, right_operand, kept_mask, product_kind):
    full_mask = expand_mask(kept_mask)
    if product_kind == "forward":
        masked = right_operand * full_mask.astype(right_operand.dtype)
        return jnp.dot(left_operand, masked, preferred_element_type=jnp.float32)
    if product_kind == "transposed":
        masked = right_operand * full_mask.astype(right_operand.dtype)
        return lax.dot_general(
            left_operand, masked, (((1,), (1,)), ((), ())), preferred_element_type=jnp.float32
        )
    product = lax.dot_general(
        left_operand, right_operand, (((0,), (0,)), ((), ())), preferred_element_type=jnp.float32
    )
    return product * full_mask.astype(jnp.float32)


def apply_blocks(left_operand, right_operand, kept_mask, product_kind):
    return dense_apply(left_operand, right_operand, kept_mask, product_kind)


def on_device(tokens, cotangent, w_gate, w_up, w_down, order_gate, order_up, order_down):
    rows_here = w_gate.shape[0] // BLOCK
    cols_here = w_gate.shape[1] // BLOCK
    row_start = lax.axis_index("row") * rows_here
    col_start = lax.axis_index("col") * cols_here
    width_blocks = rows_here * lax.axis_size("row")
    hidden_blocks = cols_here * lax.axis_size("col")
    keep_gate = kept_table(order_gate, row_start, col_start, rows_here, cols_here, hidden_blocks)
    keep_up = kept_table(order_up, row_start, col_start, rows_here, cols_here, hidden_blocks)
    keep_down = kept_table(order_down, col_start, row_start, cols_here, rows_here, width_blocks)
    tokens_all = lax.all_gather(tokens, "col", axis=0, tiled=True)
    gate_term = apply_blocks(tokens_all, w_gate, keep_gate, "forward")
    up_term = apply_blocks(tokens_all, w_up, keep_up, "forward")
    gate, up = (
        lax.psum_scatter(gate_term, "row", scatter_dimension=0, tiled=True),
        lax.psum_scatter(up_term, "row", scatter_dimension=0, tiled=True),
    )
    sigmoid_gate = jax.nn.sigmoid(gate)
    activation = gate * sigmoid_gate
    hidden = (activation * up).astype(jnp.bfloat16)
    hidden_all = lax.all_gather(hidden, "row", axis=0, tiled=True)
    output_term = apply_blocks(hidden_all, w_down, keep_down, "forward")
    output = lax.psum_scatter(output_term, "col", scatter_dimension=0, tiled=True).astype(
        jnp.bfloat16
    )
    cotangent_all = lax.all_gather(cotangent, "col", axis=0, tiled=True)
    hidden_term = apply_blocks(cotangent_all, w_down, keep_down, "transposed")
    hidden_grad = lax.psum_scatter(hidden_term, "row", scatter_dimension=0, tiled=True)
    gate_grad = (hidden_grad * up * sigmoid_gate * (1.0 + gate * (1.0 - sigmoid_gate))).astype(
        jnp.bfloat16
    )
    up_grad = (hidden_grad * activation).astype(jnp.bfloat16)
    gate_grad_all, up_grad_all = (
        lax.all_gather(gate_grad, "row", axis=0, tiled=True),
        lax.all_gather(up_grad, "row", axis=0, tiled=True),
    )
    down_weight_grad = apply_blocks(hidden_all, cotangent_all, keep_down, "weights")
    gate_weight_grad = apply_blocks(tokens_all, gate_grad_all, keep_gate, "weights")
    up_weight_grad = apply_blocks(tokens_all, up_grad_all, keep_up, "weights")
    through_gate = apply_blocks(gate_grad_all, w_gate, keep_gate, "transposed")
    through_up = apply_blocks(up_grad_all, w_up, keep_up, "transposed")
    gate_share = lax.psum_scatter(through_gate, "col", scatter_dimension=0, tiled=True)
    up_share = lax.psum_scatter(through_up, "col", scatter_dimension=0, tiled=True)
    input_grad = gate_share + up_share
    return (
        output,
        input_grad.astype(jnp.bfloat16),
        gate_weight_grad,
        up_weight_grad,
        down_weight_grad,
    )


def solution(mesh):
    placed = (
        P("col", "row"),
        P("col", "row"),
        P("row", "col"),
        P("row", "col"),
        P("col", "row"),
        P(),
        P(),
        P(),
    )
    return jax.shard_map(
        on_device,
        mesh=mesh,
        in_specs=placed,
        out_specs=(
            P("col", "row"),
            P("col", "row"),
            P("row", "col"),
            P("row", "col"),
            P("col", "row"),
        ),
        check_vma=False,
    )
```

profile of v0, /device:TPU:2, one launch (start us, length us, event | category | flops | bytes accessed | tf_op | source)
XLA Modules:
  0.0 445.8 jit_solution(2200922386354329133)
XLA Ops:
  7.2 0.7 all-gather.5.cloned.1.call-update
  7.9 0.7 all-gather.3.cloned.1.call-update
  8.7 0.7 slice.11
  9.4 0.1 broadcast_add_fusion
  9.5 0.2 compare_reduce_fusion
  9.7 0.3 broadcast_in_dim.8
  10.1 0.3 copy.50
  10.3 50.4 %all-gather.5.cloned.1.call-done = bf16[512,1024]{1,0:T(8,128)(2,1)} async-done(((bf16[16,1024]{1,0:T(8,128)(2,1)}), bf16[512,1024]{1,0:T(8,128)(2,1)}) %all-gather.5.cloned.1.call-update) | async-done | bytes 1048592 | tf_op jit(solution)/shard_map/all_gather | solution.py:68
  60.8 2.3 convolution_bitcast_fusion
  63.1 1.3 copy.46
  64.4 0.0 reduce-scatter.16.cloned.1.call-start
  64.5 0.1 broadcast_add_fusion.1
  64.5 0.2 compare_reduce_fusion.2
  64.8 0.3 broadcast_in_dim.6
  65.1 0.3 copy.48
  65.4 0.5 copy.31
  65.9 44.4 %all-gather.3.cloned.1.call-done = bf16[512,1024]{1,0:T(8,128)(2,1)} async-done(((bf16[16,1024]{1,0:T(8,128)(2,1)}), bf16[512,1024]{1,0:T(8,128)(2,1)}) %all-gather.3.cloned.1.call-update) | async-done | bytes 1048592 | tf_op jit(solution)/shard_map/all_gather | solution.py:53
  110.3 2.0 convolution_bitcast_fusion.2
  112.3 1.3 copy.42
  113.6 0.0 reduce-scatter.18.cloned.1.call-start
  113.7 0.3 broadcast_in_dim.7
  114.0 0.3 copy.49
  114.3 1.7 copy.34
  116.0 2.9 convolution_bitcast_fusion.1
  118.9 2.5 copy.44
  121.5 0.0 reduce-scatter.12.cloned.1.call-start
  121.6 30.7 %reduce-scatter.20.cloned.1.call-done = f32[64,512]{1,0:T(8,128)} async-done(((f32[512,512]{1,0:T(8,128)}), f32[64,512]{1,0:T(8,128)}) %reduce-scatter.20.cloned.1.call-update) | async-done | bytes 131088 | tf_op jit(solution)/shard_map/reduce_scatter | solution.py:70
  152.3 40.6 %reduce-scatter.16.cloned.1.call-done = f32[64,512]{1,0:T(8,128)} async-done(((f32[512,512]{1,0:T(8,128)}), f32[64,512]{1,0:T(8,128)}) %reduce-scatter.16.cloned.1.call-update) | async-done | bytes 131088 | tf_op jit(solution)/shard_map/reduce_scatter | solution.py:57
  192.9 40.0 %reduce-scatter.18.cloned.1.call-done = f32[64,512]{1,0:T(8,128)} async-done(((f32[512,512]{1,0:T(8,128)}), f32[64,512]{1,0:T(8,128)}) %reduce-scatter.18.cloned.1.call-update) | async-done | bytes 131088 | tf_op jit(solution)/shard_map/reduce_scatter | solution.py:58
  232.9 1.1 multiply_convert_fusion
  234.1 25.5 %all_gather.16 = bf16[512,512]{1,0:T(8,128)(2,1)S(1)} all-gather(bf16[64,512]{1,0:T(8,128)(2,1)S(1)} %get-tuple-element.29), channel_id=1, replica_groups=mesh['row'=8,'col'=32] {'row'}, dimensions={0}, use_global_device_ids=true | all-gather | bytes 589824 | tf_op jit(solution)/shard_map/all_gather | solution.py:63
  259.6 3.3 fusion.1
  262.9 0.0 reduce-scatter.14.cloned.1.call-start
  262.9 25.5 %all_gather.18 = bf16[512,512]{1,0:T(8,128)(2,1)S(1)} all-gather(bf16[64,512]{1,0:T(8,128)(2,1)S(1)} %get-tuple-element.28), channel_id=1, replica_groups=mesh['row'=8,'col'=32] {'row'}, dimensions={0}, use_global_device_ids=true | all-gather | bytes 589824 | tf_op jit(solution)/shard_map/all_gather | solution.py:76
  288.4 25.2 %all_gather.19 = bf16[512,512]{1,0:T(8,128)(2,1)S(1)} all-gather(bf16[64,512]{1,0:T(8,128)(2,1)S(1)} %get-tuple-element.27), channel_id=1, replica_groups=mesh['row'=8,'col'=32] {'row'}, dimensions={0}, use_global_device_ids=true | all-gather | bytes 589824 | tf_op jit(solution)/shard_map/all_gather | solution.py:77
  313.7 2.0 fusion.9
  315.7 2.1 convolution_add_fusion
  317.8 1.0 copy-done.8
  318.8 0.4 copy-done.11
  319.1 2.0 bitcast_select_fusion.1
  321.2 3.0 copy.40
  324.2 2.1 bitcast_select_fusion
  326.2 3.0 copy.41
  329.2 2.0 convolution_select_fusion
  331.3 16.4 %reduce-scatter.12.cloned.1.call-done = f32[16,1024]{1,0:T(8,128)} async-done(((f32[512,1024]{1,0:T(8,128)}), f32[16,1024]{1,0:T(8,128)}) %reduce-scatter.12.cloned.1.call-update) | async-done | bytes 65552 | tf_op jit(solution)/shard_map/reduce_scatter | solution.py:65
  347.7 1.5 convert_element_type.11
  349.1 88.4 %reduce-scatter.14.cloned.1.call-done = f32[16,1024]{1,0:T(8,128)} async-done(((f32[512,1024]{1,0:T(8,128)}), f32[16,1024]{1,0:T(8,128)}) %reduce-scatter.14.cloned.1.call-update) | async-done | bytes 65552 | tf_op jit(solution)/shard_map/reduce_scatter | solution.py:84
  437.5 1.5 convert_element_type.28
  (36 shorter events, 0.3 us)
Async XLA Ops:
  7.2 53.6 %all-gather.5.cloned.1.call-start = ((), (), s32[]{:S(2)}) async-start(), calls=%async_computation.7 | async-start | bytes 1081344 | tf_op jit(solution)/shard_map/all_gather | solution.py:68
  7.9 102.4 %all-gather.3.cloned.1.call-start = ((), (), s32[]{:S(2)}) async-start(), calls=%async_computation.5 | async-start | bytes 1081344 | tf_op jit(solution)/shard_map/all_gather | solution.py:53
  8.6 143.6 %reduce-scatter.20.cloned.1.call-start = ((), (), s32[]{:S(2)}) async-start(), calls=%async_computation.11 | async-start | bytes 1179648 | tf_op jit(solution)/shard_map/reduce_scatter | solution.py:70
  10.3 249.3 %copy-start.5 = (pred[64,8,4,256]{3,1,2,0:T(8,128)(4,1)}, pred[64,8,4,256]{3,1,2,0:T(8,128)(4,1)S(1)}, u32[]{:S(2)}) copy-start(pred[64,8,4,256]{3,1,2,0:T(8,128)(4,1)S(1)} %copy.50) | copy-start | bytes 1572868
  63.0 1.5 slice-start
  63.1 1.5 slice-start.1
  63.1 2.3 copy-start.9
  64.4 128.5 %reduce-scatter.16.cloned.1.call-start = ((), (), s32[]{:S(2)}) async-start(), calls=%async_computation.9 | async-start | bytes 1179648 | tf_op jit(solution)/shard_map/reduce_scatter | solution.py:57
  65.4 46.9 %copy-start.7 = (pred[64,8,4,256]{3,1,2,0:T(8,128)(4,1)}, pred[64,8,4,256]{3,1,2,0:T(8,128)(4,1)S(1)}, u32[]{:S(2)}) copy-start(pred[64,8,4,256]{3,1,2,0:T(8,128)(4,1)S(1)} %copy.48) | copy-start | bytes 1572868
  113.6 119.3 %reduce-scatter.18.cloned.1.call-start = ((), (), s32[]{:S(2)}) async-start(), calls=%async_computation.10 | async-start | bytes 1179648 | tf_op jit(solution)/shard_map/reduce_scatter | solution.py:58
  114.3 4.6 %copy-start = (pred[64,8,4,256]{3,1,2,0:T(8,128)(4,1)}, pred[64,8,4,256]{3,1,2,0:T(8,128)(4,1)S(1)}, u32[]{:S(2)}) copy-start(pred[64,8,4,256]{3,1,2,0:T(8,128)(4,1)S(1)} %copy.49) | copy-start | bytes 1572868
  121.5 226.2 %reduce-scatter.12.cloned.1.call-start = ((), (), s32[]{:S(2)}) async-start(), calls=%async_computation.6 | async-start | bytes 2162688 | tf_op jit(solution)/shard_map/reduce_scatter | solution.py:65
  262.9 174.6 %reduce-scatter.14.cloned.1.call-start = ((), (), s32[]{:S(2)}) async-start(), calls=%async_computation.8 | async-start | bytes 2162688 | tf_op jit(solution)/shard_map/reduce_scatter | solution.py:84
  313.7 2.0 copy-start.3
  313.7 2.0 copy-start.1
  317.7 1.0 copy-start.8
  317.7 1.4 copy-start.11
  321.2 3.0 copy-start.2
  321.2 3.0 copy-start.4
  326.2 3.0 copy-start.6
  326.2 3.0 copy-start.10
Sparse Core Ops, SparseCore 0:
  10.5 50.1 all-gather.4
  63.3 46.9 all-gather.2
  113.4 38.7 reduce-scatter.19
  155.2 37.6 reduce-scatter.15
  195.3 37.6 reduce-scatter.17
  263.0 84.6 reduce-scatter.11
  351.5 85.9 reduce-scatter.13
where the time goes:
time: 446 us
  waiting for transfers between devices  312 us (70%)
  blocking collectives  76.2 us (17%)
  matrix products  20.7 us (5%)
  local copies, waits for them, and re-layouts  17.3 us (4%)
  between operations  14.3 us (3%)
  other arithmetic  4.62 us (1%)
    reduce_scatter x1, waiting for transfers between devices, on_device(): lax.psum_scatter(through_gate, 'col', scatter_dimension=0, tiled=True)  88.4 us
    all_gather x1, waiting for transfers between devices, on_device(): cotangent_all = lax.all_gather(cotangent, 'col', axis=0, tiled=True)  50.4 us
    all_gather x1, waiting for transfers between devices, on_device(): tokens_all = lax.all_gather(tokens, 'col', axis=0, tiled=True)  44.4 us
    reduce_scatter x1, waiting for transfers between devices, on_device(): lax.psum_scatter(gate_term, 'row', scatter_dimension=0, tiled=True)  40.6 us
    reduce_scatter x1, waiting for transfers between devices, on_device(): lax.psum_scatter(up_term, 'row', scatter_dimension=0, tiled=True)  40 us
    reduce_scatter x1, waiting for transfers between devices, on_device(): lax.psum_scatter(hidden_term, 'row', scatter_dimension=0, tiled=True)  30.7 us
    all_gather x1, blocking collectives, on_device(): hidden_all = lax.all_gather(hidden, 'row', axis=0, tiled=True)  25.5 us
    all_gather x1, blocking collectives, on_device(): lax.all_gather(gate_grad, 'row', axis=0, tiled=True)  25.5 us
  transfers between devices with their start and end apart: 7, of which 7 were waited for; matrix products, arithmetic and copies ran while one was open for 8% of the time, Pallas kernels for 0%

commit v1 on v0

--- a/solution.py
+++ b/solution.py
@@ -1,9 +1,29 @@
+import functools
 import jax
 import jax.numpy as jnp
 from jax import lax
 from jax.sharding import PartitionSpec as P
+from jax.lax import axis_index, axis_size, ppermute
 
 BLOCK = 256
+
+
+def edges_update(packet, across, out_dim):
+    n_axis = axis_size(across)
+    parts_seen = [(src_i, (src_i + 1) % n_axis) for src_i in range(n_axis)]
+    xs_all = [(src_i, (src_i - 1) % n_axis) for src_i in range(n_axis)]
+    carry_out, row_out = ([packet], [packet])
+    for _ in range(n_axis // 2):
+        carry_out.append(ppermute(carry_out[-1], across, parts_seen))
+    for _ in [*range((n_axis - 1) // 2)]:
+        aux = ppermute(row_out[-1], across, xs_all)
+        row_out.append(aux)
+    g_now = jnp.concatenate([*carry_out[::-1], *row_out[1:]], axis=out_dim)
+    tall = jnp.roll(g_now, (axis_index(across) - n_axis // 2) * packet.shape[out_dim], out_dim)
+    return tall
+
+
+close_inputs = functools.partial(edges_update, across="row", out_dim=0)
 
 
 def kept_table(order, row_first, col_first, row_count, col_count, stride):
@@ -60,7 +80,7 @@
     sigmoid_gate = jax.nn.sigmoid(gate)
     activation = gate * sigmoid_gate
     hidden = (activation * up).astype(jnp.bfloat16)
-    hidden_all = lax.all_gather(hidden, "row", axis=0, tiled=True)
+    hidden_all = close_inputs(hidden)
     output_term = apply_blocks(hidden_all, w_down, keep_down, "forward")
     output = lax.psum_scatter(output_term, "col", scatter_dimension=0, tiled=True).astype(
         jnp.bfloat16

time: 446 us -> 473 us (1.061)
  waiting for transfers between devices: 312 us -> 354 us
  blocking collectives: 76.2 us -> 51.1 us
  starting transfers between devices: 0.28 us -> 10.3 us
    reduce_scatter x1, waiting for transfers between devices: 16.4 us -> 88.4 us  [on_device(): lax.psum_scatter(output_term, 'col', scatter_dimension=0, tiled=True)]
    reduce_scatter x1, waiting for transfers between devices: 88.4 us -> 46.1 us  [on_device(): lax.psum_scatter(through_gate, 'col', scatter_dimension=0, tiled=True)]
    all_gather x1 -> x0, blocking collectives: 25.5 us -> none  [on_device(): hidden_all = lax.all_gather(hidden, 'row', axis=0, tiled=True)]
    ppermute x0 -> x7, waiting for transfers between devices: none -> 12 us  [the longest x4 12 us: edges_update(): carry_out.append(ppermute(carry_out[-1], across, parts_seen))]
    ppermute x0 -> x7, starting transfers between devices: none -> 10 us  [the longest x3 9.7 us: edges_update(): aux = ppermute(row_out[-1], across, xs_all)]
    unnamed x34 -> x43, local copies, waits for them, and re-layouts: 15.5 us -> 15.2 us
  transfers between devices with their start and end apart: 7 -> 14, of which waited for: 7 -> 11; matrix products, arithmetic and copies ran while one was open for 8% -> 7% of each run, Pallas kernels for 0% -> 0%
where the time goes in v1:
time: 473 us; the launch traced here: 472 us
  waiting for transfers between devices  354 us (75%)
  blocking collectives  51.1 us (11%)
  matrix products  20.5 us (4%)
  local copies, waits for them, and re-layouts  16.9 us (4%)
  between operations  14.4 us (3%)
  starting transfers between devices  10.3 us (2%)
    reduce_scatter x1, waiting for transfers between devices, on_device(): lax.psum_scatter(output_term, 'col', scatter_dimension=0, tiled=True)  88.4 us
    all_gather x1, waiting for transfers between devices, on_device(): cotangent_all = lax.all_gather(cotangent, 'col', axis=0, tiled=True)  50.4 us
    reduce_scatter x1, waiting for transfers between devices, on_device(): lax.psum_scatter(through_gate, 'col', scatter_dimension=0, tiled=True)  46.1 us
    all_gather x1, waiting for transfers between devices, on_device(): tokens_all = lax.all_gather(tokens, 'col', axis=0, tiled=True)  44.4 us
    reduce_scatter x1, waiting for transfers between devices, on_device(): lax.psum_scatter(gate_term, 'row', scatter_dimension=0, tiled=True)  40.6 us
    reduce_scatter x1, waiting for transfers between devices, on_device(): lax.psum_scatter(up_term, 'row', scatter_dimension=0, tiled=True)  40 us
    reduce_scatter x1, waiting for transfers between devices, on_device(): lax.psum_scatter(hidden_term, 'row', scatter_dimension=0, tiled=True)  30.9 us
    all_gather x1, blocking collectives, on_device(): lax.all_gather(up_grad, 'row', axis=0, tiled=True)  25.6 us
  transfers between devices with their start and end apart: 14, of which 11 were waited for; matrix products, arithmetic and copies ran while one was open for 7% of the time, Pallas kernels for 0%

profile of v1, /device:TPU:2, one launch (start us, length us, event | category | flops | bytes accessed | tf_op | source)
XLA Modules:
  0.0 472.2 jit_solution(70404814825232081)
XLA Ops:
  7.2 0.7 all-gather.5.cloned.1.call-update
  7.9 0.7 all-gather.3.cloned.1.call-update
  8.7 0.7 slice.11
  9.7 0.3 broadcast_in_dim.8
  10.1 0.3 copy.48
  10.3 50.4 %all-gather.5.cloned.1.call-done = bf16[512,1024]{1,0:T(8,128)(2,1)} async-done(((bf16[16,1024]{1,0:T(8,128)(2,1)}), bf16[512,1024]{1,0:T(8,128)(2,1)}) %all-gather.5.cloned.1.call-update) | async-done | bytes 1048592 | tf_op jit(solution)/shard_map/all_gather | solution.py:88
  60.8 2.3 convolution_bitcast_fusion
  63.1 1.3 copy.44
  64.8 0.3 broadcast_in_dim.6
  65.1 0.3 copy.46
  65.4 0.5 copy.29
  66.0 44.4 %all-gather.3.cloned.1.call-done = bf16[512,1024]{1,0:T(8,128)(2,1)} async-done(((bf16[16,1024]{1,0:T(8,128)(2,1)}), bf16[512,1024]{1,0:T(8,128)(2,1)}) %all-gather.3.cloned.1.call-update) | async-done | bytes 1048592 | tf_op jit(solution)/shard_map/all_gather | solution.py:73
  110.3 2.0 convolution_bitcast_fusion.2
  112.3 1.3 copy.40
  113.7 0.3 broadcast_in_dim.7
  114.0 0.3 copy.47
  114.3 1.5 copy.32
  115.8 2.9 convolution_bitcast_fusion.1
  118.7 2.5 copy.42
  121.4 30.9 %reduce-scatter.20.cloned.1.call-done = f32[64,512]{1,0:T(8,128)} async-done(((f32[512,512]{1,0:T(8,128)}), f32[64,512]{1,0:T(8,128)}) %reduce-scatter.20.cloned.1.call-update) | async-done | bytes 131088 | tf_op jit(solution)/shard_map/reduce_scatter | solution.py:90
  152.3 40.6 %reduce-scatter.16.cloned.1.call-done = f32[64,512]{1,0:T(8,128)} async-done(((f32[512,512]{1,0:T(8,128)}), f32[64,512]{1,0:T(8,128)}) %reduce-scatter.16.cloned.1.call-update) | async-done | bytes 131088 | tf_op jit(solution)/shard_map/reduce_scatter | solution.py:77
  192.9 40.0 %reduce-scatter.18.cloned.1.call-done = f32[64,512]{1,0:T(8,128)} async-done(((f32[512,512]{1,0:T(8,128)}), f32[64,512]{1,0:T(8,128)}) %reduce-scatter.18.cloned.1.call-update) | async-done | bytes 131088 | tf_op jit(solution)/shard_map/reduce_scatter | solution.py:78
  233.0 1.1 multiply_convert_fusion
  234.1 25.6 %all_gather.14 = bf16[512,512]{1,0:T(8,128)(2,1)S(1)} all-gather(bf16[64,512]{1,0:T(8,128)(2,1)S(1)} %get-tuple-element.28), channel_id=1, replica_groups=mesh['row'=8,'col'=32] {'row'}, dimensions={0}, use_global_device_ids=true | all-gather | bytes 589824 | tf_op jit(solution)/shard_map/all_gather | solution.py:96
  259.6 1.8 fusion.9
  261.4 25.6 %all_gather.15 = bf16[512,512]{1,0:T(8,128)(2,1)S(1)} all-gather(bf16[64,512]{1,0:T(8,128)(2,1)S(1)} %get-tuple-element.27), channel_id=1, replica_groups=mesh['row'=8,'col'=32] {'row'}, dimensions={0}, use_global_device_ids=true | all-gather | bytes 589824 | tf_op jit(solution)/shard_map/all_gather | solution.py:97
  286.9 2.1 convolution_add_fusion
  289.1 0.3 collective-permute-start
  289.4 5.3 %collective-permute-done = bf16[64,512]{1,0:T(8,128)(2,1)S(1)} collective-permute-done((bf16[64,512]{1,0:T(8,128)(2,1)S(1)}, bf16[64,512]{1,0:T(8,128)(2,1)S(1)}, u32[]{:S(2)}, u32[]{:S(2)}) %collective-permute-start) | collective-permute-done | bytes 65568 | tf_op jit(solution)/shard_map/ppermute | solution.py:17
  294.7 3.2 collective-permute-start.4
  297.9 2.2 collective-permute-done.1
  300.1 3.2 collective-permute-start.5
  303.4 2.2 collective-permute-done.2
  305.6 3.2 collective-permute-start.6
  308.9 2.2 collective-permute-done.3
  311.3 1.0 copy-done.6
  312.3 2.0 fusion.1
  314.4 1.0 copy-done.1
  315.4 0.4 copy-done.8
  315.7 2.0 bitcast_select_fusion.1
  317.8 2.9 copy.38
  320.7 2.0 bitcast_select_fusion
  322.7 1.8 copy.39
  324.5 3.4 convolution_select_fusion
  327.9 46.1 %reduce-scatter.14.cloned.1.call-done = f32[16,1024]{1,0:T(8,128)} async-done(((f32[512,1024]{1,0:T(8,128)}), f32[16,1024]{1,0:T(8,128)}) %reduce-scatter.14.cloned.1.call-update) | async-done | bytes 65552 | tf_op jit(solution)/shard_map/reduce_scatter | solution.py:104
  374.0 1.5 convert_element_type.28
  375.5 88.4 %reduce-scatter.12.cloned.1.call-done = f32[16,1024]{1,0:T(8,128)} async-done(((f32[512,1024]{1,0:T(8,128)}), f32[16,1024]{1,0:T(8,128)}) %reduce-scatter.12.cloned.1.call-update) | async-done | bytes 65552 | tf_op jit(solution)/shard_map/reduce_scatter | solution.py:85
  463.9 1.5 convert_element_type.11
  (59 shorter events, 1.1 us)
Async XLA Ops:
  7.2 53.6 %all-gather.5.cloned.1.call-start = ((), (), s32[]{:S(2)}) async-start(), calls=%async_computation.7 | async-start | bytes 1081344 | tf_op jit(solution)/shard_map/all_gather | solution.py:88
  7.9 102.4 %all-gather.3.cloned.1.call-start = ((), (), s32[]{:S(2)}) async-start(), calls=%async_computation.5 | async-start | bytes 1081344 | tf_op jit(solution)/shard_map/all_gather | solution.py:73
  8.6 143.6 %reduce-scatter.20.cloned.1.call-start = ((), (), s32[]{:S(2)}) async-start(), calls=%async_computation.11 | async-start | bytes 1179648 | tf_op jit(solution)/shard_map/reduce_scatter | solution.py:90
  10.3 52.7 %copy-start.3 = (pred[64,8,4,256]{3,1,2,0:T(8,128)(4,1)}, pred[64,8,4,256]{3,1,2,0:T(8,128)(4,1)S(1)}, u32[]{:S(2)}) copy-start(pred[64,8,4,256]{3,1,2,0:T(8,128)(4,1)S(1)} %copy.48) | copy-start | bytes 1572868
  63.1 1.5 slice-start
  63.1 1.5 slice-start.1
  63.1 2.3 copy-start.2
  64.4 128.5 %reduce-scatter.16.cloned.1.call-start = ((), (), s32[]{:S(2)}) async-start(), calls=%async_computation.9 | async-start | bytes 1179648 | tf_op jit(solution)/shard_map/reduce_scatter | solution.py:77
  65.4 48.3 %copy-start = (pred[64,8,4,256]{3,1,2,0:T(8,128)(4,1)}, pred[64,8,4,256]{3,1,2,0:T(8,128)(4,1)S(1)}, u32[]{:S(2)}) copy-start(pred[64,8,4,256]{3,1,2,0:T(8,128)(4,1)S(1)} %copy.46) | copy-start | bytes 1572868
  113.6 119.3 %reduce-scatter.18.cloned.1.call-start = ((), (), s32[]{:S(2)}) async-start(), calls=%async_computation.10 | async-start | bytes 1179648 | tf_op jit(solution)/shard_map/reduce_scatter | solution.py:78
  121.3 252.7 %reduce-scatter.14.cloned.1.call-start = ((), (), s32[]{:S(2)}) async-start(), calls=%async_computation.8 | async-start | bytes 2162688 | tf_op jit(solution)/shard_map/reduce_scatter | solution.py:104
  289.0 23.3 %copy-start.4 = (pred[64,8,4,256]{3,1,2,0:T(8,128)(4,1)S(1)}, pred[64,8,4,256]{3,1,2,0:T(8,128)(4,1)}, u32[]{:S(2)}) copy-start(pred[64,8,4,256]{3,1,2,0:T(8,128)(4,1)} %copy-done.3) | copy-start | bytes 1572868
  289.1 174.8 %reduce-scatter.12.cloned.1.call-start = ((), (), s32[]{:S(2)}) async-start(), calls=%async_computation.6 | async-start | bytes 2162688 | tf_op jit(solution)/shard_map/reduce_scatter | solution.py:85
  289.1 5.6 %collective-permute-start = (bf16[64,512]{1,0:T(8,128)(2,1)S(1)}, bf16[64,512]{1,0:T(8,128)(2,1)S(1)}, u32[]{:S(2)}, u32[]{:S(2)}) collective-permute-start(bf16[64,512]{1,0:T(8,128)(2,1)S(1)} %get-tuple-element.29), channel_id=1, source_target_pairs={{0,32},{32,64},{64,96},{96,128},{128,160},{160,192},{192,224},{224... | collective-permute-start | bytes 196616 | tf_op jit(solution)/shard_map/ppermute | solution.py:17
  294.7 5.5 %collective-permute-start.1 = (bf16[64,512]{1,0:T(8,128)(2,1)S(1)}, bf16[64,512]{1,0:T(8,128)(2,1)S(1)}, u32[]{:S(2)}, u32[]{:S(2)}) collective-permute-start(bf16[64,512]{1,0:T(8,128)(2,1)S(1)} %collective-permute-done), channel_id=1, source_target_pairs={{0,32},{32,64},{64,96},{96,128},{128,160},{160,192},{192,224},{224... | collective-permute-start | bytes 196616 | tf_op jit(solution)/shard_map/ppermute | solution.py:17
  294.7 5.5 %collective-permute-start.4 = (bf16[64,512]{1,0:T(8,128)(2,1)S(1)}, bf16[64,512]{1,0:T(8,128)(2,1)S(1)}, u32[]{:S(2)}, u32[]{:S(2)}) collective-permute-start(bf16[64,512]{1,0:T(8,128)(2,1)S(1)} %get-tuple-element.29), channel_id=1, source_target_pairs={{0,224},{32,0},{64,32},{96,64},{128,96},{160,128},{192,160},{224,1... | collective-permute-start | bytes 196616 | tf_op jit(solution)/shard_map/ppermute | solution.py:19
  300.1 5.5 %collective-permute-start.2 = (bf16[64,512]{1,0:T(8,128)(2,1)S(1)}, bf16[64,512]{1,0:T(8,128)(2,1)S(1)}, u32[]{:S(2)}, u32[]{:S(2)}) collective-permute-start(bf16[64,512]{1,0:T(8,128)(2,1)S(1)} %collective-permute-done.1), channel_id=1, source_target_pairs={{0,32},{32,64},{64,96},{96,128},{128,160},{160,192},{192,224},{224... | collective-permute-start | bytes 196616 | tf_op jit(solution)/shard_map/ppermute | solution.py:17
  300.1 5.5 %collective-permute-start.5 = (bf16[64,512]{1,0:T(8,128)(2,1)S(1)}, bf16[64,512]{1,0:T(8,128)(2,1)S(1)}, u32[]{:S(2)}, u32[]{:S(2)}) collective-permute-start(bf16[64,512]{1,0:T(8,128)(2,1)S(1)} %collective-permute-done.4), channel_id=1, source_target_pairs={{0,224},{32,0},{64,32},{96,64},{128,96},{160,128},{192,160},{224,1... | collective-permute-start | bytes 196616 | tf_op jit(solution)/shard_map/ppermute | solution.py:19
  305.6 5.5 %collective-permute-start.3 = (bf16[64,512]{1,0:T(8,128)(2,1)S(1)}, bf16[64,512]{1,0:T(8,128)(2,1)S(1)}, u32[]{:S(2)}, u32[]{:S(2)}) collective-permute-start(bf16[64,512]{1,0:T(8,128)(2,1)S(1)} %collective-permute-done.2), channel_id=1, source_target_pairs={{0,32},{32,64},{64,96},{96,128},{128,160},{160,192},{192,224},{224... | collective-permute-start | bytes 196616 | tf_op jit(solution)/shard_map/ppermute | solution.py:17
  305.6 6.7 %copy-start.7 = (bf16[512,1024]{1,0:T(8,128)(2,1)S(1)}, bf16[512,1024]{1,0:T(8,128)(2,1)}, u32[]{:S(2)}) copy-start(bf16[512,1024]{1,0:T(8,128)(2,1)} %param.12) | copy-start | bytes 3145732
  305.6 5.6 %collective-permute-start.6 = (bf16[64,512]{1,0:T(8,128)(2,1)S(1)}, bf16[64,512]{1,0:T(8,128)(2,1)S(1)}, u32[]{:S(2)}, u32[]{:S(2)}) collective-permute-start(bf16[64,512]{1,0:T(8,128)(2,1)S(1)} %collective-permute-done.5), channel_id=1, source_target_pairs={{0,224},{32,0},{64,32},{96,64},{128,96},{160,128},{192,160},{224,1... | collective-permute-start | bytes 196616 | tf_op jit(solution)/shard_map/ppermute | solution.py:19
  311.3 1.0 copy-start.6
  314.3 1.1 copy-start.1
  314.3 1.4 copy-start.8
  322.6 1.8 copy-start.5
Sparse Core Ops, SparseCore 0:
  10.5 50.1 all-gather.4
  63.3 46.9 all-gather.2
  113.4 38.7 reduce-scatter.19
  155.2 37.6 reduce-scatter.15
  195.3 37.6 reduce-scatter.17
  289.2 84.7 reduce-scatter.13
  377.8 85.9 reduce-scatter.11
